TPU v7x, 32 devices: a whole 2x2x4 slice. The times are simulated.
32 devices in a mesh: cuts: 2 (over x), mode: 16 (over z, y, core).
Axes of the slice: x: 2, y: 2, z: 4, core: 2. Of those that a mesh axis runs over, the one named last changes fastest.
Arguments:
- stem_blocks: bfloat16 [2, 4096, 2, 256], P('cuts', 'mode'), may hold values from -6 to 6
- w1_table: bfloat16 [8, 2, 256, 256], replicated, may hold values from -0.25 to 0.25
- w2_table: bfloat16 [8, 2, 256, 256], replicated, may hold values from -0.125 to 0.125
- slice_ids: int32 [2, 2, 2], P('cuts'), may hold values from 0 to 7, as said below
- mode_perm: int32 [256], replicated, may hold values from 0 to 255, each once
Outputs:
- amplitudes: float32 [256, 16, 2, 256], P('mode', 'cuts')
Inputs may be any that keep to these rules, and one draw needn't show every extreme that they name: For each stem block b, the 2 values slice_ids[:,b,0] are distinct, and so are the 2 values slice_ids[:,b,1]. `mode_perm`: each column appears once.
All inputs are finite; a program needn't handle non-finite values.
Results may differ from a plain program's by a relative error of at most 0.0029.
Values may be sent and summed in bfloat16 or wider, within the bound.
No kernel may reach another device: no remote copies, remote signals or barrier semaphores. Data moves between devices by JAX's collectives and lax.ppermute only.
A program may use at most 64 MiB of HBM per device.

v0:
```python
import jax
import jax.numpy as jnp
from jax import lax
from jax.sharding import PartitionSpec as P


def broadcast(block, axis, source):
    block = jnp.where(lax.axis_index(axis) == source, block, jnp.zeros_like(block))
    return lax.psum(block, axis)


def widen_first(entry):
    real_part, imag_part = (entry[0], entry[1])
    upper = jnp.concatenate([real_part, imag_part], axis=1)
    lower = jnp.concatenate([-imag_part, real_part], axis=1)
    return jnp.concatenate([upper, lower], axis=0)


def widen_second(entry):
    real_part, imag_part = (entry[0], entry[1])
    first_row = jnp.concatenate([real_part, imag_part], axis=1)
    second_row = jnp.concatenate([-imag_part, real_part], axis=1)
    return jnp.stack([first_row, second_row], axis=0)


def second_step(exchanged, weight_two, contract_cols, free_cols):
    block_count, mode_count, piece_rows, _ = exchanged.shape
    pieces = exchanged.reshape(block_count, mode_count, piece_rows, 2, contract_cols, free_cols)
    wide_out = weight_two.shape[3]
    shaped = weight_two.reshape(block_count, 2, mode_count, contract_cols, wide_out)
    return jnp.einsum("nhqpcs,nphco->qso", pieces, shaped, preferred_element_type=jnp.float32)


def on_device(stem_blocks, w1_table, w2_table, slice_ids, mode_perm):
    mode_count = lax.axis_size("mode")
    row_count = stem_blocks.shape[1]
    stem_width = stem_blocks.shape[3]
    mid_width = w1_table.shape[3]
    inner_width = w2_table.shape[2]
    out_width = w2_table.shape[3]
    piece_rows = row_count // mode_count
    contract_cols = inner_width // mode_count
    free_cols = mid_width // contract_cols
    block_count = slice_ids.shape[1]
    first_all = jax.vmap(widen_first)(jnp.take(w1_table, mode_perm, axis=3))
    second_all = jax.vmap(widen_second)(w2_table)
    own_slices = slice_ids[0]
    begin = jnp.zeros((piece_rows, free_cols, 2 * out_width), jnp.float32)

    def one_block(block_index, running):
        stem_part = broadcast(stem_blocks[0], "cuts", block_index)
        slice_pair = own_slices[block_index]
        weight_one = lax.dynamic_index_in_dim(first_all, slice_pair[0], 0, keepdims=False)
        product = jnp.dot(
            stem_part.reshape(row_count, 2 * stem_width),
            weight_one,
            preferred_element_type=jnp.float32,
        ).astype(jnp.bfloat16)
        exchanged = lax.all_to_all(
            product[None, None], "mode", split_axis=2, concat_axis=1, tiled=True
        )
        weight_two = lax.dynamic_index_in_dim(second_all, slice_pair[1], 0, keepdims=True)
        return running + second_step(exchanged, weight_two, contract_cols, free_cols)

    amplitude = lax.fori_loop(0, block_count, one_block, begin)
    summed = lax.psum_scatter(amplitude, "cuts", scatter_dimension=1, tiled=True)
    return summed.reshape(piece_rows, summed.shape[1], 2, out_width)


def solution(mesh):
    placed = (P("cuts", "mode", None, None), P(), P(), P("cuts", None, None), P())
    return jax.shard_map(
        on_device,
        mesh=mesh,
        in_specs=placed,
        out_specs=P("mode", "cuts", None, None),
        check_vma=False,
    )
```

profile of v0, /device:TPU:0, one launch (start us, length us, event | category | flops | bytes accessed | tf_op | source)
XLA Modules:
  0.0 173.1 jit_solution(13787529332660151836)
XLA Ops:
  7.4 3.2 %slice_bitcast_fusion.2 = (bf16[8,256,256]{2,1,0:T(8,128)(2,1)}, bf16[8,256,256]{2,1,0:T(8,128)(2,1)}) fusion(bf16[8,2,256,256]{3,2,1,0:T(8,128)(2,1)} %param.9), kind=kLoop, calls=%fused_computation.19 | loop fusion | bytes 4194304 | tf_op jit(solution)/shard_map/vmap()/squeeze | solution.py:20
  10.6 1.1 fusion.6
  11.7 0.9 copy-done.6
  12.6 3.1 %copy.29 = bf16[8,2,256,256]{2,0,3,1:T(8,128)(2,1)} copy(bf16[8,2,256,256]{3,2,1,0:T(8,128)(2,1)S(1)} %copy-done.6) | data formatting | bytes 4194304 | tf_op args[1]
  15.7 2.4 %gather_fusion = bf16[256,8,2,256]{3,1,2,0:T(8,128)(2,1)S(1)} fusion(bf16[8,2,256,256]{2,0,3,1:T(8,128)(2,1)} %copy.29, s32[1024]{0:T(1024)S(1)} %pad_clamp_fusion), kind=kCustom, calls=%fused_computation | custom fusion | bytes 4195328 | tf_op jit(solution)/shard_map/jit(_take)/gather | solution.py:45
  18.1 0.9 select_bitcast_fusion
  19.0 1.1 slice_bitcast_fusion
  20.2 13.0 %maximum_maximum_fusion = bf16[8,512,512]{1,0,2:T(8,128)(2,1)} fusion(bf16[8,256,256]{1,0,2:T(8,128)(2,1)} %get-tuple-element.171, bf16[8,256,256]{1,0,2:T(8,128)(2,1)S(1)} %fusion.7, bf16[8,256,256]{1,0,2:T(8,128)(2,1)S(1)} %get-tuple-element.170), kind=kLoop, calls=%fused_computation.12 | loop fusion | flops 16777216 | bytes 7340032 | tf_op jit(solution)/shard_map/vmap()/concatenate | solution.py:16
  33.3 7.7 %copy.34 = bf16[8,512,512]{2,1,0:T(8,128)(2,1)} copy(bf16[8,512,512]{1,0,2:T(8,128)(2,1)} %maximum_maximum_fusion) | data formatting | bytes 8388608
  41.0 1.9 %maximum_bitcast_fusion.1 = (bf16[1,8,256,512]{3,2,0,1:T(8,128)(2,1)S(1)}, bf16[1,8,256,512]{3,2,0,1:T(8,128)(2,1)S(1)}) fusion(bf16[8,256,256]{2,1,0:T(8,128)(2,1)S(1)} %copy-done.5, bf16[8,256,256]{2,1,0:T(8,128)(2,1)} %get-tuple-element.169, bf16[8,256,256]{2,1,0:T(8,128)(2,1)S(1)} %copy-done.4), kind=kLoop, calls=%fused_computation.14 | loop fusion | flops 8388608 | bytes 7340032 | tf_op jit(solution)/shard_map/vmap()/stack | solution.py:23
  42.9 2.3 %maximum_bitcast_fusion = bf16[8,2,256,512]{3,2,1,0:T(8,128)(2,1)} fusion(bf16[1,8,256,512]{3,2,0,1:T(8,128)(2,1)S(1)} %get-tuple-element.173, bf16[1,8,256,512]{3,2,0,1:T(8,128)(2,1)S(1)} %get-tuple-element.172), kind=kLoop, calls=%fused_computation.13 | loop fusion | flops 2097152 | bytes 8388608 | tf_op jit(solution)/shard_map/vmap()/transpose | solution.py:46
  45.3 104.0 %while.14 = (s32[]{:T(128)}, f32[16,16,512]{2,1,0:T(8,128)S(1)}, bf16[1,256,2,256]{3,2,1,0:T(2,128)(2,1)S(1)}, s32[2,2]{1,0:T(2,128)S(1)}, bf16[8,512,512]{2,1,0...) while((s32[]{:T(128)}, f32[16,16,512]{2,1,0:T(8,128)S(1)}, ...), condition=%wide.region_2.3_spmd.clone, body=%wide.region_0.0_spmd.clone.sunk | while | flops 269090816 | bytes 11534731 | solution.py:65
  48.9 25.5 %all-reduce.2.cloned.1.call-done = bf16[256,512]{1,0:T(8,128)(2,1)} async-done(((bf16[256,512]{1,0:T(8,128)(2,1)}), bf16[256,512]{1,0:T(8,128)(2,1)}) %all-reduce.2.cloned.1.call-update) | async-done | bytes 262160 | tf_op jit(solution)/shard_map/while/body/eval_jaxpr/psum | solution.py:9
  74.4 1.4 fusion.23
  76.7 2.2 %reduce.6 = bf16[256,512]{1,0:T(8,128)(2,1)S(1)} reduce(bf16[256,1,1,512]{3,2,1,0:T(2,128)(2,1)S(1)} %bitcast.79, bf16[]{:T(256)} %broadcast.40), dimensions={1,2}, to_apply=%bitcast.54.reduce_sub_computation | reduce | bytes 524290 | tf_op jit(solution)/shard_map/while
  79.0 0.9 reshape.66
  79.8 5.6 %all-to-all-start = ((bf16[16,2,4096]{2,1,0:T(2,128)(2,1)}), bf16[16,2,4096]{2,1,0:T(2,128)(2,1)S(1)}, u32[]{:S(2)}, u32[]{:S(2)}) async-start(bf16[16,2,4096]{2,1,0:T(2,128)(2,1)} %reshape.66), calls=%async_computation | async-start | bytes 524288 | tf_op jit(solution)/shard_map/while/body/eval_jaxpr/all_to_all | solution.py:59
  87.5 1.1 constant_dynamic-slice_fusion.5
  88.6 6.9 %all-to-all-done = bf16[16,2,4096]{2,1,0:T(2,128)(2,1)S(1)} async-done(((bf16[16,2,4096]{2,1,0:T(2,128)(2,1)}), bf16[16,2,4096]{2,1,0:T(2,128)(2,1)S(1)}, u32[]{:S(2)}, u32[]{:S(2)}) %all-to-all-start) | async-done | bytes 262176 | tf_op jit(solution)/shard_map/while/body/eval_jaxpr/all_to_all | solution.py:59
  95.8 1.5 bitcast_reduce_fusion.2
  97.3 1.7 reshape.68
  103.5 20.2 %all-reduce.2.cloned.1.call-done = bf16[256,512]{1,0:T(8,128)(2,1)} async-done(((bf16[256,512]{1,0:T(8,128)(2,1)}), bf16[256,512]{1,0:T(8,128)(2,1)}) %all-reduce.2.cloned.1.call-update) | async-done | bytes 262160 | tf_op jit(solution)/shard_map/while/body/eval_jaxpr/psum | solution.py:9
  123.7 1.4 fusion.23
  126.1 2.2 %reduce.6 = bf16[256,512]{1,0:T(8,128)(2,1)S(1)} reduce(bf16[256,1,1,512]{3,2,1,0:T(2,128)(2,1)S(1)} %bitcast.79, bf16[]{:T(256)} %broadcast.40), dimensions={1,2}, to_apply=%bitcast.54.reduce_sub_computation | reduce | bytes 524290 | tf_op jit(solution)/shard_map/while
  128.3 0.9 reshape.66
  129.2 5.6 %all-to-all-start = ((bf16[16,2,4096]{2,1,0:T(2,128)(2,1)}), bf16[16,2,4096]{2,1,0:T(2,128)(2,1)S(1)}, u32[]{:S(2)}, u32[]{:S(2)}) async-start(bf16[16,2,4096]{2,1,0:T(2,128)(2,1)} %reshape.66), calls=%async_computation | async-start | bytes 524288 | tf_op jit(solution)/shard_map/while/body/eval_jaxpr/all_to_all | solution.py:59
  136.9 1.1 constant_dynamic-slice_fusion.5
  138.0 6.9 %all-to-all-done = bf16[16,2,4096]{2,1,0:T(2,128)(2,1)S(1)} async-done(((bf16[16,2,4096]{2,1,0:T(2,128)(2,1)}), bf16[16,2,4096]{2,1,0:T(2,128)(2,1)S(1)}, u32[]{:S(2)}, u32[]{:S(2)}) %all-to-all-start) | async-done | bytes 262176 | tf_op jit(solution)/shard_map/while/body/eval_jaxpr/all_to_all | solution.py:59
  145.1 1.5 bitcast_reduce_fusion.2
  146.6 1.7 reshape.68
  150.1 13.7 %reduce-scatter.2.cloned.1.call-done = f32[16,8,512]{2,1,0:T(8,128)} async-done(((f32[16,16,512]{2,1,0:T(8,128)}), f32[16,8,512]{2,1,0:T(8,128)}) %reduce-scatter.2.cloned.1.call-update) | async-done | bytes 262160 | tf_op jit(solution)/shard_map/reduce_scatter | solution.py:66
  163.8 1.8 %reshape.44 = f32[16,8,2,256]{3,2,1,0:T(2,128)} reshape(f32[16,8,512]{2,1,0:T(8,128)} %reduce-scatter.2.cloned.1.call-done) | data formatting | bytes 524288 | tf_op jit(solution)/shard_map/reshape | solution.py:67
  (46 shorter events, 8.5 us)
Async XLA Ops:
  7.4 3.2 %copy-start.3 = (bf16[8,2,256,256]{3,2,1,0:T(8,128)(2,1)S(1)}, bf16[8,2,256,256]{3,2,1,0:T(8,128)(2,1)}, u32[]{:S(2)}) copy-start(bf16[8,2,256,256]{3,2,1,0:T(8,128)(2,1)} %param.9) | copy-start | bytes 6291460
  7.4 4.3 %copy-start.7 = (s32[256]{0:T(256)S(1)}, s32[256]{0:T(256)}, u32[]{:S(2)}) copy-start(s32[256]{0:T(256)} %param.11) | copy-start | bytes 3076
  10.6 2.0 %copy-start.6 = (bf16[8,2,256,256]{3,2,1,0:T(8,128)(2,1)S(1)}, bf16[8,2,256,256]{3,2,1,0:T(8,128)(2,1)}, u32[]{:S(2)}) copy-start(bf16[8,2,256,256]{3,2,1,0:T(8,128)(2,1)} %param.8) | copy-start | bytes 6291460
  33.3 7.7 %copy-start.4 = (bf16[8,256,256]{2,1,0:T(8,128)(2,1)S(1)}, bf16[8,256,256]{2,1,0:T(8,128)(2,1)}, u32[]{:S(2)}) copy-start(bf16[8,256,256]{2,1,0:T(8,128)(2,1)} %fusion.6) | copy-start | bytes 3145732
  33.3 7.7 %copy-start.5 = (bf16[8,256,256]{2,1,0:T(8,128)(2,1)S(1)}, bf16[8,256,256]{2,1,0:T(8,128)(2,1)}, u32[]{:S(2)}) copy-start(bf16[8,256,256]{2,1,0:T(8,128)(2,1)} %get-tuple-element.168) | copy-start | bytes 3145732
  42.9 2.4 %copy-start.1 = (bf16[1,256,2,256]{3,2,1,0:T(2,128)(2,1)S(1)}, bf16[1,256,2,256]{3,2,1,0:T(2,128)(2,1)}, u32[]{:S(2)}) copy-start(bf16[1,256,2,256]{3,2,1,0:T(2,128)(2,1)} %param.7) | copy-start | bytes 786436
  42.9 2.4 %copy-start.8 = (s32[1,2,2]{2,1,0:T(2,128)S(1)}, s32[1,2,2]{2,1,0:T(2,128)}, u32[]{:S(2)}) copy-start(s32[1,2,2]{2,1,0:T(2,128)} %param.10) | copy-start | bytes 52
  45.3 29.1 %all-reduce.2.cloned.1.call-start = ((), (), s32[]{:S(2)}) async-start(), calls=%async_computation.3 | async-start | bytes 524288 | tf_op jit(solution)/shard_map/while/body/eval_jaxpr/psum | solution.py:9
  79.8 15.7 %all-to-all-start = ((bf16[16,2,4096]{2,1,0:T(2,128)(2,1)}), bf16[16,2,4096]{2,1,0:T(2,128)(2,1)S(1)}, u32[]{:S(2)}, u32[]{:S(2)}) async-start(bf16[16,2,4096]{2,1,0:T(2,128)(2,1)} %reshape.66), calls=%async_computation | async-start | bytes 524288 | tf_op jit(solution)/shard_map/while/body/eval_jaxpr/all_to_all | solution.py:59
  99.0 1.0 copy-start.2
  99.9 23.8 %all-reduce.2.cloned.1.call-start = ((), (), s32[]{:S(2)}) async-start(), calls=%async_computation.3 | async-start | bytes 524288 | tf_op jit(solution)/shard_map/while/body/eval_jaxpr/psum | solution.py:9
  129.2 15.7 %all-to-all-start = ((bf16[16,2,4096]{2,1,0:T(2,128)(2,1)}), bf16[16,2,4096]{2,1,0:T(2,128)(2,1)S(1)}, u32[]{:S(2)}, u32[]{:S(2)}) async-start(bf16[16,2,4096]{2,1,0:T(2,128)(2,1)} %reshape.66), calls=%async_computation | async-start | bytes 524288 | tf_op jit(solution)/shard_map/while/body/eval_jaxpr/all_to_all | solution.py:59
  148.3 1.0 copy-start.2
  149.3 0.8 copy-start
  149.3 14.5 %reduce-scatter.2.cloned.1.call-start = ((), (), s32[]{:S(2)}) async-start(), calls=%async_computation.2 | async-start | bytes 786432 | tf_op jit(solution)/shard_map/reduce_scatter | solution.py:66
Sparse Core Ops, SparseCore 0:
  48.5 25.8 all-reduce.1
  103.1 20.5 all-reduce.1
Sparse Core Ops, SparseCore 1:
  152.0 11.8 reduce-scatter.1
where the time goes:
time: 174 us; the launch traced here: 173 us
  waiting for transfers between devices  73.3 us (42%)
  local copies, waits for them, and re-layouts  37 us (21%)
  other arithmetic  24.2 us (14%)
  between operations  14.9 us (9%)
  starting transfers between devices  11.3 us (6%)
  loops' own time  8.19 us (5%)
  matrix products  4.28 us (2%)
    psum x2, waiting for transfers between devices, broadcast(): return lax.psum(block, axis)  45.7 us
    all_to_all x2, waiting for transfers between devices, one_block(): lax.all_to_all(product[None, None], 'mode', split_axis=2, concat_axis=1,...  13.8 us
    reduce_scatter x1, waiting for transfers between devices, on_device(): lax.psum_scatter(amplitude, 'cuts', scatter_dimension=1, tiled=True)  13.7 us
    concatenate x1, other arithmetic, widen_first(): return jnp.concatenate([upper, lower], axis=0)  13 us
    unnamed x18, local copies, waits for them, and re-layouts  12.5 us
    all_to_all x2, starting transfers between devices, one_block(): lax.all_to_all(product[None, None], 'mode', split_axis=2, concat_axis=1,...  11.2 us
    another operation x1, loops' own time, on_device(): amplitude = lax.fori_loop(0, block_count, one_block, begin)  8.19 us
    while x12, local copies, waits for them, and re-layouts  5.23 us
  transfers between devices with their start and end apart: 5, of which 5 were waited for; matrix products, arithmetic and copies ran while one was open for 2% of the time, Pallas kernels for 0%

commit v1 on v0

--- a/solution.py
+++ b/solution.py
@@ -1,7 +1,18 @@
+import functools
 import jax
 import jax.numpy as jnp
 from jax import lax
 from jax.sharding import PartitionSpec as P
+
+
+def shape_shelves_over_axis(z_in, comm_axis):
+    return jnp.concatenate(
+        lax.all_to_all(jnp.stack(jnp.split(z_in, lax.psum(1, comm_axis), axis=2)), comm_axis, 0, 0),
+        1,
+    )
+
+
+point_bench = functools.partial(shape_shelves_over_axis, comm_axis="mode")
 
 
 def broadcast(block, axis, source):
@@ -56,9 +67,7 @@
             weight_one,
             preferred_element_type=jnp.float32,
         ).astype(jnp.bfloat16)
-        exchanged = lax.all_to_all(
-            product[None, None], "mode", split_axis=2, concat_axis=1, tiled=True
-        )
+        exchanged = point_bench(product[None, None])
         weight_two = lax.dynamic_index_in_dim(second_all, slice_pair[1], 0, keepdims=True)
         return running + second_step(exchanged, weight_two, contract_cols, free_cols)
 

time: 174 us -> 182 us (1.046)
  local copies, waits for them, and re-layouts: 37 us -> 49.3 us
  other arithmetic: 24.2 us -> 19.8 us
    while x12 -> x36, local copies, waits for them, and re-layouts: 5.23 us -> 20.1 us
    while x2 -> x0, other arithmetic: 4.41 us -> none
    all_to_all x2 -> x0, local copies, waits for them, and re-layouts: 2.98 us -> none  [one_block(): lax.all_to_all(product[None, None], 'mode', split_axis=2, concat_axis=1,...]
    another operation x2 -> x4, local copies, waits for them, and re-layouts: 3.38 us -> 4.56 us
where the time goes in v1:
time: 182 us; the launch traced here: 181 us
  waiting for transfers between devices  74.1 us (41%)
  local copies, waits for them, and re-layouts  49.3 us (27%)
  other arithmetic  19.8 us (11%)
  between operations  14.9 us (8%)
  starting transfers between devices  11.2 us (6%)
  loops' own time  7.34 us (4%)
  matrix products  4.28 us (2%)
    psum x2, waiting for transfers between devices, broadcast(): return lax.psum(block, axis)  46.2 us
    while x36, local copies, waits for them, and re-layouts  20.1 us
    all_to_all x2, waiting for transfers between devices, shape_shelves_over_axis(): lax.all_to_all(jnp.stack(jnp.split(z_in, lax.psum(1, comm_axis), axis=2))...  14.2 us
    reduce_scatter x1, waiting for transfers between devices, on_device(): lax.psum_scatter(amplitude, 'cuts', scatter_dimension=1, tiled=True)  13.7 us
    concatenate x1, other arithmetic, widen_first(): return jnp.concatenate([upper, lower], axis=0)  13.1 us
    unnamed x18, local copies, waits for them, and re-layouts  12.6 us
    all_to_all x2, starting transfers between devices, shape_shelves_over_axis(): lax.all_to_all(jnp.stack(jnp.split(z_in, lax.psum(1, comm_axis), axis=2))...  11.2 us
    another operation x1, loops' own time, on_device(): amplitude = lax.fori_loop(0, block_count, one_block, begin)  7.34 us
  transfers between devices with their start and end apart: 5, of which 5 were waited for; matrix products, arithmetic and copies ran while one was open for 2% of the time, Pallas kernels for 0%

profile of v1, /device:TPU:0, one launch (start us, length us, event | category | flops | bytes accessed | tf_op | source)
XLA Modules:
  0.0 181.0 jit_solution(142036293469523483)
XLA Ops:
  7.4 3.2 %slice_bitcast_fusion.18 = (bf16[8,256,256]{2,1,0:T(8,128)(2,1)}, bf16[8,256,256]{2,1,0:T(8,128)(2,1)}) fusion(bf16[8,2,256,256]{3,2,1,0:T(8,128)(2,1)} %param.9), kind=kLoop, calls=%fused_computation.51 | loop fusion | bytes 4194304 | tf_op jit(solution)/shard_map/vmap()/squeeze | solution.py:31
  10.6 1.0 fusion.6
  11.7 0.9 copy-done.6
  12.6 3.1 %copy.12 = bf16[8,2,256,256]{2,0,3,1:T(8,128)(2,1)} copy(bf16[8,2,256,256]{3,2,1,0:T(8,128)(2,1)S(1)} %copy-done.6) | data formatting | bytes 4194304 | tf_op args[1]
  15.7 2.4 %gather_fusion = bf16[256,8,2,256]{3,1,2,0:T(8,128)(2,1)S(1)} fusion(bf16[8,2,256,256]{2,0,3,1:T(8,128)(2,1)} %copy.12, s32[1024]{0:T(1024)S(1)} %pad_clamp_fusion), kind=kCustom, calls=%fused_computation | custom fusion | bytes 4195328 | tf_op jit(solution)/shard_map/jit(_take)/gather | solution.py:56
  18.1 0.9 select_bitcast_fusion
  19.1 1.1 slice_bitcast_fusion.16
  20.2 13.1 %maximum_maximum_fusion = bf16[8,512,512]{1,0,2:T(8,128)(2,1)} fusion(bf16[8,256,256]{1,0,2:T(8,128)(2,1)} %get-tuple-element.159, bf16[8,256,256]{1,0,2:T(8,128)(2,1)S(1)} %fusion.7, bf16[8,256,256]{1,0,2:T(8,128)(2,1)S(1)} %get-tuple-element.158), kind=kLoop, calls=%fused_computation.44 | loop fusion | flops 16777216 | bytes 7340032 | tf_op jit(solution)/shard_map/vmap()/concatenate | solution.py:27
  33.3 7.8 %copy.17 = bf16[8,512,512]{2,1,0:T(8,128)(2,1)} copy(bf16[8,512,512]{1,0,2:T(8,128)(2,1)} %maximum_maximum_fusion) | data formatting | bytes 8388608
  41.1 1.9 %maximum_bitcast_fusion.1 = (bf16[1,8,256,512]{3,2,0,1:T(8,128)(2,1)S(1)}, bf16[1,8,256,512]{3,2,0,1:T(8,128)(2,1)S(1)}) fusion(bf16[8,256,256]{2,1,0:T(8,128)(2,1)S(1)} %copy-done.5, bf16[8,256,256]{2,1,0:T(8,128)(2,1)} %get-tuple-element.157, bf16[8,256,256]{2,1,0:T(8,128)(2,1)S(1)} %copy-done.4), kind=kLoop, calls=%fused_computation.46 | loop fusion | flops 8388608 | bytes 7340032 | tf_op jit(solution)/shard_map/vmap()/stack | solution.py:34
  43.0 2.3 %maximum_bitcast_fusion = bf16[8,2,256,512]{3,2,1,0:T(8,128)(2,1)} fusion(bf16[1,8,256,512]{3,2,0,1:T(8,128)(2,1)S(1)} %get-tuple-element.161, bf16[1,8,256,512]{3,2,0,1:T(8,128)(2,1)S(1)} %get-tuple-element.160), kind=kLoop, calls=%fused_computation.45 | loop fusion | flops 2097152 | bytes 8388608 | tf_op jit(solution)/shard_map/vmap()/transpose | solution.py:57
  45.4 111.8 %while.14 = (s32[]{:T(128)}, f32[16,16,512]{2,1,0:T(8,128)S(1)}, bf16[1,256,2,256]{3,2,1,0:T(2,128)(2,1)S(1)}, s32[2,2]{1,0:T(2,128)S(1)}, bf16[8,512,512]{2,1,0...) while((s32[]{:T(128)}, f32[16,16,512]{2,1,0:T(8,128)S(1)}, ...), condition=%wide.region_2.3_spmd.clone, body=%wide.region_0.0_spmd.clone.sunk | while | flops 269090816 | bytes 9437565 | solution.py:74
  45.6 0.7 copy.32
  46.4 0.6 fusion.22
  48.7 25.8 %all-reduce.2.cloned.1.call-done = bf16[256,512]{1,0:T(8,128)(2,1)} async-done(((bf16[256,512]{1,0:T(8,128)(2,1)}), bf16[256,512]{1,0:T(8,128)(2,1)}) %all-reduce.2.cloned.1.call-update) | async-done | bytes 262160 | tf_op jit(solution)/shard_map/while/body/eval_jaxpr/psum | solution.py:20
  74.5 1.4 fusion.23
  85.6 5.6 %all-to-all-start = ((bf16[16,1,1,16,512]{4,3,2,1,0:T(8,128)(2,1)}), bf16[16,1,1,16,512]{4,3,2,1,0:T(8,128)(2,1)S(1)}, u32[]{:S(2)}, u32[]{:S(2)}) async-start(bf16[16,1,1,16,512]{4,3,2,1,0:T(8,128)(2,1)} %constant_dynamic-update-slice_fusion.47), calls=%async_computation | async-start | bytes 524288 | tf_op jit(solution)/shard_map/while/body/eval_jaxpr/all_to_all | solution.py:10
  93.1 1.1 constant_dynamic-slice_fusion.5
  94.2 7.1 %all-to-all-done = bf16[16,1,1,16,512]{4,3,2,1,0:T(8,128)(2,1)S(1)} async-done(((bf16[16,1,1,16,512]{4,3,2,1,0:T(8,128)(2,1)}), bf16[16,1,1,16,512]{4,3,2,1,0:T(8,128)(2,1)S(1)}, u32[]{:S(2)}, u32[]{:S(2)}) %all-to-all-start) | async-done | bytes 262176 | tf_op jit(solution)/shard_map/while/body/eval_jaxpr/all_to_all | solution.py:10
  101.3 1.7 reshape.57
  103.0 0.7 fusion.24
  104.1 0.7 copy.32
  107.3 20.4 %all-reduce.2.cloned.1.call-done = bf16[256,512]{1,0:T(8,128)(2,1)} async-done(((bf16[256,512]{1,0:T(8,128)(2,1)}), bf16[256,512]{1,0:T(8,128)(2,1)}) %all-reduce.2.cloned.1.call-update) | async-done | bytes 262160 | tf_op jit(solution)/shard_map/while/body/eval_jaxpr/psum | solution.py:20
  127.7 1.4 fusion.23
  138.9 5.6 %all-to-all-start = ((bf16[16,1,1,16,512]{4,3,2,1,0:T(8,128)(2,1)}), bf16[16,1,1,16,512]{4,3,2,1,0:T(8,128)(2,1)S(1)}, u32[]{:S(2)}, u32[]{:S(2)}) async-start(bf16[16,1,1,16,512]{4,3,2,1,0:T(8,128)(2,1)} %constant_dynamic-update-slice_fusion.47), calls=%async_computation | async-start | bytes 524288 | tf_op jit(solution)/shard_map/while/body/eval_jaxpr/all_to_all | solution.py:10
  146.4 1.1 constant_dynamic-slice_fusion.5
  147.5 7.1 %all-to-all-done = bf16[16,1,1,16,512]{4,3,2,1,0:T(8,128)(2,1)S(1)} async-done(((bf16[16,1,1,16,512]{4,3,2,1,0:T(8,128)(2,1)}), bf16[16,1,1,16,512]{4,3,2,1,0:T(8,128)(2,1)S(1)}, u32[]{:S(2)}, u32[]{:S(2)}) %all-to-all-start) | async-done | bytes 262176 | tf_op jit(solution)/shard_map/while/body/eval_jaxpr/all_to_all | solution.py:10
  154.5 1.7 reshape.57
  156.2 0.7 fusion.24
  157.2 0.8 copy-done
  158.0 13.7 %reduce-scatter.2.cloned.1.call-done = f32[16,8,512]{2,1,0:T(8,128)} async-done(((f32[16,16,512]{2,1,0:T(8,128)}), f32[16,8,512]{2,1,0:T(8,128)}) %reduce-scatter.2.cloned.1.call-update) | async-done | bytes 262160 | tf_op jit(solution)/shard_map/reduce_scatter | solution.py:75
  171.7 1.8 %reshape.40 = f32[16,8,2,256]{3,2,1,0:T(2,128)} reshape(f32[16,8,512]{2,1,0:T(8,128)} %reduce-scatter.2.cloned.1.call-done) | data formatting | bytes 524288 | tf_op jit(solution)/shard_map/reshape | solution.py:76
  (66 shorter events, 21.1 us)
Async XLA Ops:
  7.4 3.3 %copy-start.3 = (bf16[8,2,256,256]{3,2,1,0:T(8,128)(2,1)S(1)}, bf16[8,2,256,256]{3,2,1,0:T(8,128)(2,1)}, u32[]{:S(2)}) copy-start(bf16[8,2,256,256]{3,2,1,0:T(8,128)(2,1)} %param.9) | copy-start | bytes 6291460
  7.4 4.3 %copy-start.7 = (s32[256]{0:T(256)S(1)}, s32[256]{0:T(256)}, u32[]{:S(2)}) copy-start(s32[256]{0:T(256)} %param.11) | copy-start | bytes 3076
  10.6 2.0 %copy-start.6 = (bf16[8,2,256,256]{3,2,1,0:T(8,128)(2,1)S(1)}, bf16[8,2,256,256]{3,2,1,0:T(8,128)(2,1)}, u32[]{:S(2)}) copy-start(bf16[8,2,256,256]{3,2,1,0:T(8,128)(2,1)} %param.8) | copy-start | bytes 6291460
  33.3 7.8 %copy-start.4 = (bf16[8,256,256]{2,1,0:T(8,128)(2,1)S(1)}, bf16[8,256,256]{2,1,0:T(8,128)(2,1)}, u32[]{:S(2)}) copy-start(bf16[8,256,256]{2,1,0:T(8,128)(2,1)} %fusion.6) | copy-start | bytes 3145732
  33.3 7.8 %copy-start.5 = (bf16[8,256,256]{2,1,0:T(8,128)(2,1)S(1)}, bf16[8,256,256]{2,1,0:T(8,128)(2,1)}, u32[]{:S(2)}) copy-start(bf16[8,256,256]{2,1,0:T(8,128)(2,1)} %get-tuple-element.156) | copy-start | bytes 3145732
  43.0 2.4 %copy-start.1 = (bf16[1,256,2,256]{3,2,1,0:T(2,128)(2,1)S(1)}, bf16[1,256,2,256]{3,2,1,0:T(2,128)(2,1)}, u32[]{:S(2)}) copy-start(bf16[1,256,2,256]{3,2,1,0:T(2,128)(2,1)} %param.7) | copy-start | bytes 786436
  43.0 2.4 %copy-start.8 = (s32[1,2,2]{2,1,0:T(2,128)S(1)}, s32[1,2,2]{2,1,0:T(2,128)}, u32[]{:S(2)}) copy-start(s32[1,2,2]{2,1,0:T(2,128)} %param.10) | copy-start | bytes 52
  45.4 29.1 %all-reduce.2.cloned.1.call-start = ((), (), s32[]{:S(2)}) async-start(), calls=%async_computation.3 | async-start | bytes 524288 | tf_op jit(solution)/shard_map/while/body/eval_jaxpr/psum | solution.py:20
  85.6 15.7 %all-to-all-start = ((bf16[16,1,1,16,512]{4,3,2,1,0:T(8,128)(2,1)}), bf16[16,1,1,16,512]{4,3,2,1,0:T(8,128)(2,1)S(1)}, u32[]{:S(2)}, u32[]{:S(2)}) async-start(bf16[16,1,1,16,512]{4,3,2,1,0:T(8,128)(2,1)} %constant_dynamic-update-slice_fusion.47), calls=%async_computation | async-start | bytes 524288 | tf_op jit(solution)/shard_map/while/body/eval_jaxpr/all_to_all | solution.py:10
  103.0 1.0 copy-start.2
  103.9 23.8 %all-reduce.2.cloned.1.call-start = ((), (), s32[]{:S(2)}) async-start(), calls=%async_computation.3 | async-start | bytes 524288 | tf_op jit(solution)/shard_map/while/body/eval_jaxpr/psum | solution.py:20
  138.9 15.7 %all-to-all-start = ((bf16[16,1,1,16,512]{4,3,2,1,0:T(8,128)(2,1)}), bf16[16,1,1,16,512]{4,3,2,1,0:T(8,128)(2,1)S(1)}, u32[]{:S(2)}, u32[]{:S(2)}) async-start(bf16[16,1,1,16,512]{4,3,2,1,0:T(8,128)(2,1)} %constant_dynamic-update-slice_fusion.47), calls=%async_computation | async-start | bytes 524288 | tf_op jit(solution)/shard_map/while/body/eval_jaxpr/all_to_all | solution.py:10
  156.2 1.0 copy-start.2
  157.2 0.8 copy-start
  157.2 14.5 %reduce-scatter.2.cloned.1.call-start = ((), (), s32[]{:S(2)}) async-start(), calls=%async_computation.2 | async-start | bytes 786432 | tf_op jit(solution)/shard_map/reduce_scatter | solution.py:75
Sparse Core Ops, SparseCore 0:
  48.6 25.8 all-reduce.1
  107.1 20.5 all-reduce.1
Sparse Core Ops, SparseCore 1:
  159.9 11.8 reduce-scatter.1
